TPU v7x, 32 devices: a whole 2x2x4 slice. The times are simulated.
32 devices in a mesh: ctx: 16 (over z, x, core), fsdp: 2 (over y).
Axes of the slice: x: 2, y: 2, z: 4, core: 2. Of those that a mesh axis runs over, the one named last changes fastest.
Arguments:
- activations: bfloat16 [4096, 8192], P('ctx', 'fsdp'), may hold values from -8.5 to 8.5
- w_query: bfloat16 [8192, 8192], P('ctx', 'fsdp'), may hold values from -0.044194174 to 0.044194174
- w_key: bfloat16 [8192, 1024], P('ctx', 'fsdp'), may hold values from -0.044194174 to 0.044194174
- w_value: bfloat16 [8192, 1024], P('ctx', 'fsdp'), may hold values from -0.0625 to 0.0625
- seed_words: int32 [1], replicated, may hold values from 0 to 1073741823
- stream_offset: int32 [1], replicated, may hold values from 0 to 1048575
- layer_index: int32 [1], replicated, may hold values from 0 to 79
Outputs:
- attention: bfloat16 [4096, 8192], P('ctx', 'fsdp')
All inputs are finite; a program needn't handle non-finite values.
Results may differ from a plain program's by a relative error of at most 0.007.
Values may be sent and summed in bfloat16 or wider, within the bound.
No kernel may reach another device: no remote copies, remote signals or barrier semaphores. Data moves between devices by JAX's collectives and lax.ppermute only.
A program may use at most 320 MiB of HBM per device.

v0:
```python
import math
import jax
import jax.numpy as jnp
from jax import lax
from jax.sharding import PartitionSpec as P

HQ = 64
KV = 8
HD = 128
golden = -1640531535
drop_rate = 0.1
drop_level = 1677722
rope_theta = 500000.0
masked_score = -1e30


def shift_down(values, amount):
    return lax.shift_right_logical(values, jnp.full(values.shape, amount, jnp.int32))


def scramble(values):
    values = jnp.bitwise_xor(values, shift_down(values, 16))
    values = values * jnp.int32(-2048144789)
    values = jnp.bitwise_xor(values, shift_down(values, 13))
    values = values * jnp.int32(-1028477387)
    return jnp.bitwise_xor(values, shift_down(values, 16))


def head_word(seed_words, stream_offset, layer_index, head_ids):
    inner = scramble(head_ids + stream_offset[0])
    middle = scramble(layer_index[0] * jnp.int32(golden) + inner)
    return scramble(seed_words[0] + middle)


def keep_factor(row_words, key_positions):
    mixed_bits = scramble(row_words[:, None] + key_positions[None, :] * jnp.int32(golden))
    return shift_down(mixed_bits, 8) >= drop_level


def rotate(values, positions):
    half_width = values.shape[-1] // 2
    exponent = jnp.arange(half_width, dtype=jnp.float32) * 2.0 / values.shape[-1]
    frequency = rope_theta ** (-exponent)
    angles = positions.astype(jnp.float32)[:, None] * frequency[None, :]
    cosine = jnp.cos(angles)
    sine_part = jnp.sin(angles)
    first_half = values[..., :half_width]
    second_half = values[..., half_width:]
    return jnp.concatenate(
        [
            first_half * cosine - second_half * sine_part,
            second_half * cosine + first_half * sine_part,
        ],
        axis=-1,
    )


def shards(activations, w_query, w_key, w_value, seed_words, stream_offset, layer_index):
    ctx_count = lax.axis_size("ctx")
    ctx_place = lax.axis_index("ctx")
    fsdp_place = lax.axis_index("fsdp")
    tok_rows = activations.shape[0]
    local_heads = w_query.shape[1] // HD
    local_groups = w_key.shape[1] // HD
    splits = max(1, ctx_count // local_heads)
    owned_heads = max(1, local_heads // ctx_count)
    piece_rows = tok_rows // splits
    query_count = ctx_count * piece_rows
    full_rows = lax.all_gather(activations, "fsdp", axis=1, tiled=True)
    positions = ctx_place * tok_rows + jnp.arange(tok_rows, dtype=jnp.int32)

    def add_rows(running, weight):
        row_count = weight.shape[0]
        shaped = weight.reshape(row_count, running.shape[0], HD)
        return jnp.einsum("tn,nhe->hte", full_rows, shaped, preferred_element_type=jnp.float32)

    zero_query = jnp.zeros((local_heads, tok_rows, HD), jnp.float32)
    zero_group = jnp.zeros((local_groups, tok_rows, HD), jnp.float32)
    query_sum = add_rows(zero_query, lax.all_gather(w_query, "ctx", axis=0, tiled=True))
    key_sum = add_rows(zero_group, lax.all_gather(w_key, "ctx", axis=0, tiled=True))
    value_sum = add_rows(zero_group, lax.all_gather(w_value, "ctx", axis=0, tiled=True))
    keys = rotate(key_sum, positions).astype(jnp.bfloat16)
    values = value_sum.astype(jnp.bfloat16)
    queries = (
        rotate(query_sum, positions)
        .astype(jnp.bfloat16)
        .reshape(local_heads * splits, piece_rows, HD)
    )
    received = lax.all_to_all(queries, "ctx", split_axis=0, concat_axis=1, tiled=True)
    slots = ctx_place * owned_heads + jnp.arange(owned_heads, dtype=jnp.int32)
    head_local = slots // splits
    part_index = slots % splits
    head_global = fsdp_place * local_heads + head_local
    group_local = head_local // (HQ // KV)
    source_rows = jnp.arange(ctx_count, dtype=jnp.int32)[None, :, None] * tok_rows
    inner_rows = (
        part_index[:, None, None] * piece_rows
        + jnp.arange(piece_rows, dtype=jnp.int32)[None, None, :]
    )
    query_pos = (source_rows + inner_rows).reshape(owned_heads, query_count)
    words = head_word(seed_words, stream_offset, layer_index, head_global)
    row_words = scramble(jnp.bitwise_xor(words[:, None], query_pos))
    query_block = math.gcd(query_count, 512)
    score_scale = HD ** (-0.5)
    start_state = (
        jnp.full((owned_heads, query_count), masked_score, jnp.float32),
        jnp.zeros((owned_heads, query_count), jnp.float32),
        jnp.zeros((owned_heads, query_count, HD), jnp.float32),
    )
    key_piece = lax.all_gather(keys, "ctx", axis=1, tiled=True)
    value_piece = lax.all_gather(values, "ctx", axis=1, tiled=True)
    key_count = key_piece.shape[1]
    key_block = math.gcd(key_count, 512)
    key_steps = key_count // key_block
    block_total = query_count // query_block * key_steps
    outcomes = []
    for head_slot in range(owned_heads):
        head_keys = lax.dynamic_index_in_dim(key_piece, group_local[head_slot], 0, keepdims=False)
        head_values = lax.dynamic_index_in_dim(
            value_piece, group_local[head_slot], 0, keepdims=False
        )
        head_queries = received[head_slot]
        head_pos = query_pos[head_slot]
        head_words = row_words[head_slot]

        def advance(flat_index, state):
            query_start = flat_index // key_steps * query_block
            key_start = flat_index % key_steps * key_block
            block_pos = lax.dynamic_slice_in_dim(head_pos, query_start, query_block)
            key_pos = key_start + jnp.arange(key_block, dtype=jnp.int32)
            top_all, sum_all, accum_all = state
            block_queries = lax.dynamic_slice_in_dim(head_queries, query_start, query_block, 0)
            block_words = lax.dynamic_slice_in_dim(head_words, query_start, query_block)
            block_keys = lax.dynamic_slice_in_dim(head_keys, key_start, key_block, 0)
            block_values = lax.dynamic_slice_in_dim(head_values, key_start, key_block, 0)
            scores = (
                jnp.einsum(
                    "qe,ke->qk", block_queries, block_keys, preferred_element_type=jnp.float32
                )
                * score_scale
            )
            visible = key_pos[None, :] <= block_pos[:, None]
            old_top = lax.dynamic_slice_in_dim(top_all, query_start, query_block)
            new_top = jnp.maximum(
                old_top, jnp.max(jnp.where(visible, scores, masked_score), axis=1)
            )
            weights = jnp.where(visible, jnp.exp(scores - new_top[:, None]), 0.0)
            factor = jnp.exp(old_top - new_top)
            dropped = jnp.where(keep_factor(block_words, key_pos), weights, 0.0).astype(
                jnp.bfloat16
            )
            old_sum = lax.dynamic_slice_in_dim(sum_all, query_start, query_block)
            old_accum = lax.dynamic_slice_in_dim(accum_all, query_start, query_block, 0)
            new_sum = old_sum * factor + jnp.sum(weights, axis=1)
            new_accum = old_accum * factor[:, None] + jnp.einsum(
                "qk,ke->qe", dropped, block_values, preferred_element_type=jnp.float32
            )
            return (
                lax.dynamic_update_slice_in_dim(top_all, new_top, query_start, 0),
                lax.dynamic_update_slice_in_dim(sum_all, new_sum, query_start, 0),
                lax.dynamic_update_slice_in_dim(accum_all, new_accum, query_start, 0),
            )

        outcome = lax.fori_loop(
            0,
            block_total,
            advance,
            (start_state[0][head_slot], start_state[1][head_slot], start_state[2][head_slot]),
        )
        outcomes.append(outcome)
    top_all = jnp.stack([outcome[0] for outcome in outcomes])
    sum_all = jnp.stack([outcome[1] for outcome in outcomes])
    accum_all = jnp.stack([outcome[2] for outcome in outcomes])
    attended = (accum_all / (sum_all * (1.0 - drop_rate))[..., None]).astype(jnp.bfloat16)
    returned = lax.all_to_all(attended, "ctx", split_axis=1, concat_axis=0, tiled=True)
    return (
        returned.reshape(local_heads, tok_rows, HD)
        .transpose(1, 0, 2)
        .reshape(tok_rows, local_heads * HD)
    )


def solution(mesh):
    placed = (P("ctx", "fsdp"), P("ctx", "fsdp"), P("ctx", "fsdp"), P("ctx", "fsdp"), P(), P(), P())
    return jax.shard_map(
        shards, mesh=mesh, in_specs=placed, out_specs=P("ctx", "fsdp"), check_vma=False
    )
```

profile of v0, /device:TPU:1, one launch (start us, length us, event | category | flops | bytes accessed | tf_op | source)
XLA Modules:
  0.0 1313.4 jit_solution(4340345081472851318)
XLA Ops:
  9.7 77.2 %all-gather.11.cloned.1.call-done = bf16[8192,512]{1,0:T(8,128)(2,1)} async-done(((bf16[512,512]{1,0:T(8,128)(2,1)}), bf16[8192,512]{1,0:T(8,128)(2,1)}) %all-gather.11.cloned.1.call-update) | async-done | bytes 8388624 | tf_op jit(solution)/shard_map/all_gather | solution.py:80
  87.0 11.6 copy.45
  98.6 44.5 %all-gather.9.cloned.1.call-done = bf16[256,8192]{1,0:T(8,128)(2,1)} async-done(((bf16[256,4096]{1,0:T(8,128)(2,1)}), bf16[256,8192]{1,0:T(8,128)(2,1)}) %all-gather.9.cloned.1.call-update) | async-done | bytes 4194320 | tf_op jit(solution)/shard_map/all_gather | solution.py:69
  143.1 6.9 fusion.72
  150.9 69.7 %all-gather.15.cloned.1.call-done = bf16[8192,512]{1,0:T(8,128)(2,1)} async-done(((bf16[512,512]{1,0:T(8,128)(2,1)}), bf16[8192,512]{1,0:T(8,128)(2,1)}) %all-gather.15.cloned.1.call-update) | async-done | bytes 8388624 | tf_op jit(solution)/shard_map/all_gather | solution.py:81
  220.6 12.0 copy.47
  232.7 7.7 fusion.78
  240.4 306.1 %all-gather.7.cloned.1.call-done = bf16[8192,4096]{1,0:T(8,128)(2,1)} async-done(((bf16[512,4096]{1,0:T(8,128)(2,1)}), bf16[8192,4096]{1,0:T(8,128)(2,1)}) %all-gather.7.cloned.1.call-update) | async-done | bytes 67108880 | tf_op jit(solution)/shard_map/all_gather | solution.py:79
  546.5 87.9 %copy.43 = bf16[8192,4096]{0,1:T(8,128)(2,1)} copy(bf16[8192,4096]{1,0:T(8,128)(2,1)} %all-gather.7.cloned.1.call-done) | data formatting | bytes 134217728 | tf_op jit(solution)/shard_map/all_gather | solution.py:79
  634.4 29.1 %fusion.69 = f32[32,256,128]{1,2,0:T(8,128)} fusion(bf16[8192,32,128]{0,2,1:T(8,128)(2,1)} %bitcast, bf16[256,8192]{1,0:T(8,128)(2,1)} %all-gather.9.cloned.1.call-done), kind=kOutput, calls=%fused_computation.96 | convolution fusion | flops 17179869184 | bytes 75497472 | tf_op jit(solution)/shard_map/tn,nhe->hte/dot_general | solution.py:75
  663.5 2.9 subtract_convert_fusion
  667.9 4.7 all-to-all-start
  679.2 2.8 constant_dynamic-slice_fusion.3
  681.9 2.3 copy.50
  684.2 3.2 constant_dynamic-slice_fusion.2
  687.4 2.3 copy.51
  690.9 2.3 copy.48
  693.2 20.9 %all-to-all-done = bf16[32,256,128]{1,2,0:T(8,128)(2,1)S(1)} async-done(((bf16[32,256,128]{1,2,0:T(8,128)(2,1)}), bf16[32,256,128]{1,2,0:T(8,128)(2,1)S(1)}, u32[]{:S(2)}, u32[]{:S(2)}) %all-to-all-start) | async-done | bytes 2097184 | tf_op jit(solution)/shard_map/all_to_all | solution.py:89
  715.3 2.3 copy.49
  717.7 255.0 %while.39 = (s32[]{:T(128)}, f32[4096]{0:T(1024)S(1)}, f32[4096]{0:T(1024)S(1)}, f32[4096,128]{1,0:T(8,128)S(1)}, s32[4096]{0:T(1024)S(1)}, /*index=5*/bf16[4096...) while((s32[]{:T(128)}, f32[4096]{0:T(1024)S(1)}, ...), condition=%wide.region_7.8_spmd, body=%wide.region_4.7_spmd.sunk | while | flops 140642336 | bytes 4188568 | solution.py:164
  731.8 1.9 fusion.118
  735.8 1.9 fusion.118
  739.8 1.9 fusion.118
  743.7 1.9 fusion.118
  911.2 1.9 fusion.118
  915.2 1.9 fusion.118
  974.5 254.9 %while.38 = (s32[]{:T(128)}, f32[4096]{0:T(1024)S(1)}, f32[4096]{0:T(1024)S(1)}, f32[4096,128]{1,0:T(8,128)S(1)}, s32[4096]{0:T(1024)S(1)}, /*index=5*/bf16[4096...) while((s32[]{:T(128)}, f32[4096]{0:T(1024)S(1)}, ...), condition=%wide.region_3.4_spmd, body=%wide.region_0.3_spmd.sunk | while | flops 140642336 | bytes 4188568 | solution.py:164
  1167.9 1.9 fusion.113
  1171.9 1.9 fusion.113
  1175.9 1.9 fusion.113
  1179.9 1.9 fusion.113
  1183.8 1.9 fusion.113
  1187.8 1.9 fusion.113
  1191.8 1.9 fusion.113
  1195.8 1.9 fusion.113
  1199.7 1.9 fusion.113
  1203.7 1.9 fusion.113
  1207.7 1.9 fusion.113
  1211.7 1.9 fusion.113
  1215.6 1.9 fusion.113
  1219.6 1.9 fusion.113
  1223.6 1.9 fusion.113
  1227.6 1.9 fusion.113
  1229.5 2.0 copy.52
  1231.5 9.3 fusion.68
  1240.8 58.3 %all_to_all.33 = bf16[2,4096,128]{2,0,1:T(2,128)(2,1)S(1)} all-to-all(bf16[2,4096,128]{2,0,1:T(2,128)(2,1)S(1)} %fusion.68), channel_id=1, replica_groups=mesh['ctx'=16,'fsdp'=2] {'ctx'}, dimensions={1} | all-to-all | bytes 4194304 | tf_op jit(solution)/shard_map/all_to_all | solution.py:175
  1299.5 2.9 copy.55
  1302.4 4.1 copy.56
  (1305 shorter events, 473.4 us)
Async XLA Ops:
  6.5 80.4 %all-gather.11.cloned.1.call-start = ((), (), s32[]{:S(2)}) async-start(), calls=%async_computation.4 | async-start | bytes 8912896 | tf_op jit(solution)/shard_map/all_gather | solution.py:80
  7.3 135.8 %all-gather.9.cloned.1.call-start = ((), (), s32[]{:S(2)}) async-start(), calls=%async_computation.3 | async-start | bytes 6291456 | tf_op jit(solution)/shard_map/all_gather | solution.py:69
  8.0 212.6 %all-gather.15.cloned.1.call-start = ((), (), s32[]{:S(2)}) async-start(), calls=%async_computation.6 | async-start | bytes 8912896 | tf_op jit(solution)/shard_map/all_gather | solution.py:81
  8.7 537.7 %all-gather.7.cloned.1.call-start = ((), (), s32[]{:S(2)}) async-start(), calls=%async_computation.2 | async-start | bytes 71303168 | tf_op jit(solution)/shard_map/all_gather | solution.py:79
  9.3 669.9 %all-gather.13.cloned.1.call-start = ((), (), s32[]{:S(2)}) async-start(), calls=%async_computation.5 | async-start | bytes 4456448 | tf_op jit(solution)/shard_map/all_gather | solution.py:110
  150.9 533.3 %all-gather.17.cloned.1.call-start = ((), (), s32[]{:S(2)}) async-start(), calls=%async_computation.7 | async-start | bytes 4456448 | tf_op jit(solution)/shard_map/all_gather | solution.py:111
  667.9 46.2 %all-to-all-start = ((bf16[32,256,128]{1,2,0:T(8,128)(2,1)}), bf16[32,256,128]{1,2,0:T(8,128)(2,1)S(1)}, u32[]{:S(2)}, u32[]{:S(2)}) async-start(bf16[32,256,128]{1,2,0:T(8,128)(2,1)} %pad_maximum_fusion), calls=%async_computation | async-start | bytes 4194304 | tf_op jit(solution)/shard_map/all_to_all | solution.py:89
  972.7 1.7 copy-start
Sparse Core Ops, SparseCore 0:
  9.5 77.3 all-gather.10
  88.5 54.5 all-gather.8
  145.3 75.3 all-gather.14
  222.1 324.3 all-gather.6
  548.5 53.1 all-gather.12
  603.7 51.3 all-gather.16
where the time goes:
time: 1320 us; the launch traced here: 1310 us
  waiting for transfers between devices  521 us (39%)
  matrix products  446 us (34%)
  local copies, waits for them, and re-layouts  161 us (12%)
  other arithmetic  95.8 us (7%)
  blocking collectives  58.3 us (4%)
  between operations  19.1 us (1%)
    all_gather x1, waiting for transfers between devices, shards(): lax.all_gather(w_query, 'ctx', axis=0, tiled=True)  306 us
    dot_general x128, matrix products, advance(): jnp.einsum('qk,ke->qe', dropped, block_values, preferred_element_type=jnp...  238 us
    dot_general x128, matrix products, advance(): jnp.einsum('qe,ke->qk', block_queries, block_keys, preferred_element_type...  164 us
    all_gather x1, local copies, waits for them, and re-layouts, shards(): lax.all_gather(w_query, 'ctx', axis=0, tiled=True)  87.9 us
    all_gather x1, waiting for transfers between devices, shards(): lax.all_gather(w_key, 'ctx', axis=0, tiled=True)  77.2 us
    all_gather x1, waiting for transfers between devices, shards(): lax.all_gather(w_value, 'ctx', axis=0, tiled=True)  69.7 us
    all_to_all x1, blocking collectives, shards(): lax.all_to_all(attended, 'ctx', split_axis=1, concat_axis=0, tiled=True)  58.3 us
    all_gather x1, waiting for transfers between devices, shards(): full_rows = lax.all_gather(activations, 'fsdp', axis=1, tiled=True)  44.5 us
  transfers between devices with their start and end apart: 7, of which 5 were waited for; matrix products, arithmetic and copies ran while one was open for 13% of the time, Pallas kernels for 0%

commit v1 on v0

--- a/solution.py
+++ b/solution.py
@@ -12,6 +12,19 @@
 drop_level = 1677722
 rope_theta = 500000.0
 masked_score = -1e30
+
+
+def collect(array, axis, dim):
+    size, index, width = (lax.axis_size(axis), lax.axis_index(axis), array.shape[dim])
+    upward = [(i, (i + 1) % size) for i in range(size)]
+    out = jnp.zeros((*array.shape[:dim], size * width, *array.shape[dim + 1 :]), array.dtype)
+    carried = array
+    for step in range(size):
+        source = (index - step) % size
+        out = lax.dynamic_update_slice_in_dim(out, carried, source * width, axis=dim)
+        if step < size - 1:
+            carried = lax.ppermute(carried, axis, upward)
+    return out
 
 
 def shift_down(values, amount):
@@ -78,7 +91,7 @@
     zero_group = jnp.zeros((local_groups, tok_rows, HD), jnp.float32)
     query_sum = add_rows(zero_query, lax.all_gather(w_query, "ctx", axis=0, tiled=True))
     key_sum = add_rows(zero_group, lax.all_gather(w_key, "ctx", axis=0, tiled=True))
-    value_sum = add_rows(zero_group, lax.all_gather(w_value, "ctx", axis=0, tiled=True))
+    value_sum = add_rows(zero_group, collect(w_value, "ctx", 0))
     keys = rotate(key_sum, positions).astype(jnp.bfloat16)
     values = value_sum.astype(jnp.bfloat16)
     queries = (

time: 1320 us -> 1280 us (0.970)
  waiting for transfers between devices: 521 us -> 453 us
  local copies, waits for them, and re-layouts: 161 us -> 178 us
    ppermute x0 -> x15, waiting for transfers between devices: none -> 180 us  [collect(): carried = lax.ppermute(carried, axis, upward)]
    all_gather x1, waiting for transfers between devices: 77.2 us -> 0.02 us  [shards(): lax.all_gather(w_key, 'ctx', axis=0, tiled=True)]
    all_gather x1 -> x0, waiting for transfers between devices: 69.7 us -> none  [shards(): lax.all_gather(w_value, 'ctx', axis=0, tiled=True)]
    all_gather x1, waiting for transfers between devices: 306 us -> 251 us  [shards(): lax.all_gather(w_query, 'ctx', axis=0, tiled=True)]
    all_gather x1, waiting for transfers between devices: 44.5 us -> 0.01 us  [shards(): full_rows = lax.all_gather(activations, 'fsdp', axis=1, tiled=True)]
    dynamic_update_slice x0 -> x16, local copies, waits for them, and re-layouts: none -> 14.1 us  [collect(): lax.dynamic_update_slice_in_dim(out, carried, source * width, axis=dim)]
  transfers between devices with their start and end apart: 7 -> 21, of which waited for: 5 -> 17; matrix products, arithmetic and copies ran while one was open for 13% -> 15% of each run, Pallas kernels for 0% -> 0%
where the time goes in v1:
time: 1280 us; the launch traced here: 1270 us
  waiting for transfers between devices  453 us (35%)
  matrix products  446 us (35%)
  local copies, waits for them, and re-layouts  178 us (14%)
  other arithmetic  95.8 us (7%)
  blocking collectives  58.3 us (5%)
  between operations  19.3 us (2%)
  starting transfers between devices  15.5 us (1%)
    all_gather x1, waiting for transfers between devices, shards(): lax.all_gather(w_query, 'ctx', axis=0, tiled=True)  251 us
    dot_general x128, matrix products, advance(): jnp.einsum('qk,ke->qe', dropped, block_values, preferred_element_type=jnp...  238 us
    ppermute x15, waiting for transfers between devices, collect(): carried = lax.ppermute(carried, axis, upward)  180 us
    dot_general x128, matrix products, advance(): jnp.einsum('qe,ke->qk', block_queries, block_keys, preferred_element_type...  164 us
    all_gather x1, local copies, waits for them, and re-layouts, shards(): lax.all_gather(w_query, 'ctx', axis=0, tiled=True)  87.6 us
    all_to_all x1, blocking collectives, shards(): lax.all_to_all(attended, 'ctx', split_axis=1, concat_axis=0, tiled=True)  58.3 us
    dot_general x3, matrix products, add_rows(): jnp.einsum('tn,nhe->hte', full_rows, shaped, preferred_element_type=jnp.f...  44.3 us
    reduce_sum x128, other arithmetic, advance(): new_sum = old_sum * factor + jnp.sum(weights, axis=1)  30.5 us
  transfers between devices with their start and end apart: 21, of which 17 were waited for; matrix products, arithmetic and copies ran while one was open for 15% of the time, Pallas kernels for 0%

profile of v1, /device:TPU:1, one launch (start us, length us, event | category | flops | bytes accessed | tf_op | source)
XLA Modules:
  0.0 1273.3 jit_solution(5642730194947042380)
XLA Ops:
  8.8 2.7 collective-permute-start
  11.5 6.1 collective-permute-done
  17.6 2.5 collective-permute-start.1
  20.1 6.1 collective-permute-done.1
  26.2 2.5 collective-permute-start.2
  28.7 6.1 collective-permute-done.2
  34.8 2.5 collective-permute-start.3
  37.3 7.9 collective-permute-done.3
  45.9 10.6 collective-permute-done.4
  56.5 11.3 collective-permute-done.5
  67.8 11.3 collective-permute-done.6
  79.1 20.5 %collective-permute-done.7 = bf16[512,512]{1,0:T(8,128)(2,1)S(1)} collective-permute-done((bf16[512,512]{1,0:T(8,128)(2,1)S(1)}, bf16[512,512]{1,0:T(8,128)(2,1)S(1)}, u32[]{:S(2)}, u32[]{:S(2)}) %collective-permute-start.7) | collective-permute-done | bytes 524320 | tf_op jit(solution)/shard_map/ppermute | solution.py:26
  99.6 13.4 %collective-permute-done.8 = bf16[512,512]{1,0:T(8,128)(2,1)S(1)} collective-permute-done((bf16[512,512]{1,0:T(8,128)(2,1)S(1)}, bf16[512,512]{1,0:T(8,128)(2,1)S(1)}, u32[]{:S(2)}, u32[]{:S(2)}) %collective-permute-start.8) | collective-permute-done | bytes 524320 | tf_op jit(solution)/shard_map/ppermute | solution.py:26
  113.0 22.6 %collective-permute-done.9 = bf16[512,512]{1,0:T(8,128)(2,1)S(1)} collective-permute-done((bf16[512,512]{1,0:T(8,128)(2,1)S(1)}, bf16[512,512]{1,0:T(8,128)(2,1)S(1)}, u32[]{:S(2)}, u32[]{:S(2)}) %collective-permute-start.9) | collective-permute-done | bytes 524320 | tf_op jit(solution)/shard_map/ppermute | solution.py:26
  135.6 16.8 %collective-permute-done.10 = bf16[512,512]{1,0:T(8,128)(2,1)S(1)} collective-permute-done((bf16[512,512]{1,0:T(8,128)(2,1)S(1)}, bf16[512,512]{1,0:T(8,128)(2,1)S(1)}, u32[]{:S(2)}, u32[]{:S(2)}) %collective-permute-start.10) | collective-permute-done | bytes 524320 | tf_op jit(solution)/shard_map/ppermute | solution.py:26
  152.7 14.1 %collective-permute-done.11 = bf16[512,512]{1,0:T(8,128)(2,1)S(1)} collective-permute-done((bf16[512,512]{1,0:T(8,128)(2,1)S(1)}, bf16[512,512]{1,0:T(8,128)(2,1)S(1)}, u32[]{:S(2)}, u32[]{:S(2)}) %collective-permute-start.11) | collective-permute-done | bytes 524320 | tf_op jit(solution)/shard_map/ppermute | solution.py:26
  166.8 6.4 broadcast_in_dim.99
  189.8 16.8 %collective-permute-done.13 = bf16[512,512]{1,0:T(8,128)(2,1)} collective-permute-done((bf16[512,512]{1,0:T(8,128)(2,1)}, bf16[512,512]{1,0:T(8,128)(2,1)}, u32[]{:S(2)}, u32[]{:S(2)}) %collective-permute-start.13) | collective-permute-done | bytes 524320 | tf_op jit(solution)/shard_map/ppermute | solution.py:26
  214.0 15.3 %collective-permute-done.14 = bf16[512,512]{1,0:T(8,128)(2,1)S(1)} collective-permute-done((bf16[512,512]{1,0:T(8,128)(2,1)}, bf16[512,512]{1,0:T(8,128)(2,1)S(1)}, u32[]{:S(2)}, u32[]{:S(2)}) %collective-permute-start.14) | collective-permute-done | bytes 524320 | tf_op jit(solution)/shard_map/ppermute | solution.py:26
  230.4 8.1 fusion.78
  239.1 12.0 copy.105
  251.1 7.2 fusion.72
  259.1 251.0 %all-gather.6.cloned.1.call-done = bf16[8192,4096]{1,0:T(8,128)(2,1)} async-done(((bf16[512,4096]{1,0:T(8,128)(2,1)}), bf16[8192,4096]{1,0:T(8,128)(2,1)}) %all-gather.6.cloned.1.call-update) | async-done | bytes 67108880 | tf_op jit(solution)/shard_map/all_gather | solution.py:92
  510.1 87.6 %copy.103 = bf16[8192,4096]{0,1:T(8,128)(2,1)} copy(bf16[8192,4096]{1,0:T(8,128)(2,1)} %all-gather.6.cloned.1.call-done) | data formatting | bytes 134217728 | tf_op jit(solution)/shard_map/all_gather | solution.py:92
  597.7 29.0 %fusion.69 = f32[32,256,128]{1,2,0:T(8,128)} fusion(bf16[8192,32,128]{0,2,1:T(8,128)(2,1)} %bitcast, bf16[256,8192]{1,0:T(8,128)(2,1)} %all-gather.8.cloned.1.call-done), kind=kOutput, calls=%fused_computation.96 | convolution fusion | flops 17179869184 | bytes 75497472 | tf_op jit(solution)/shard_map/tn,nhe->hte/dot_general | solution.py:88
  626.7 2.9 subtract_convert_fusion
  631.2 3.8 all-to-all-start
  641.9 2.7 constant_dynamic-slice_fusion.2
  644.6 2.3 copy.126
  648.2 2.7 constant_dynamic-slice_fusion.3
  650.9 2.3 copy.125
  654.5 20.1 %all-to-all-done = bf16[32,256,128]{1,2,0:T(8,128)(2,1)S(1)} async-done(((bf16[32,256,128]{1,2,0:T(8,128)(2,1)}), bf16[32,256,128]{1,2,0:T(8,128)(2,1)S(1)}, u32[]{:S(2)}, u32[]{:S(2)}) %all-to-all-start) | async-done | bytes 2097184 | tf_op jit(solution)/shard_map/all_to_all | solution.py:102
  675.7 2.3 copy.124
  678.1 255.0 %while.39 = (s32[]{:T(128)}, f32[4096]{0:T(1024)S(1)}, f32[4096]{0:T(1024)S(1)}, f32[4096,128]{1,0:T(8,128)S(1)}, s32[4096]{0:T(1024)S(1)}, /*index=5*/bf16[4096...) while((s32[]{:T(128)}, f32[4096]{0:T(1024)S(1)}, ...), condition=%wide.region_7.8_spmd, body=%wide.region_4.7_spmd.sunk | while | flops 140642336 | bytes 4188568 | solution.py:177
  875.6 1.9 fusion.118
  934.9 254.8 %while.38 = (s32[]{:T(128)}, f32[4096]{0:T(1024)S(1)}, f32[4096]{0:T(1024)S(1)}, f32[4096,128]{1,0:T(8,128)S(1)}, s32[4096]{0:T(1024)S(1)}, /*index=5*/bf16[4096...) while((s32[]{:T(128)}, f32[4096]{0:T(1024)S(1)}, ...), condition=%wide.region_3.4_spmd, body=%wide.region_0.3_spmd.sunk | while | flops 140642336 | bytes 4188568 | solution.py:177
  945.0 1.9 fusion.113
  964.9 1.9 fusion.113
  984.9 1.9 fusion.113
  1004.8 1.9 fusion.113
  1024.7 1.9 fusion.113
  1044.6 1.9 fusion.113
  1064.5 1.9 fusion.113
  1189.8 2.0 copy.127
  1191.8 9.3 fusion.68
  1201.1 58.3 %all_to_all.33 = bf16[2,4096,128]{2,0,1:T(2,128)(2,1)S(1)} all-to-all(bf16[2,4096,128]{2,0,1:T(2,128)(2,1)S(1)} %fusion.68), channel_id=1, replica_groups=mesh['ctx'=16,'fsdp'=2] {'ctx'}, dimensions={1} | all-to-all | bytes 4194304 | tf_op jit(solution)/shard_map/all_to_all | solution.py:188
  1259.8 2.9 copy.130
  1262.7 4.1 copy.131
  (1390 shorter events, 526.3 us)
Async XLA Ops:
  6.5 2.3 copy-start.1
  6.5 223.9 %all-gather.8.cloned.1.call-start = ((), (), s32[]{:S(2)}) async-start(), calls=%async_computation.3 | async-start | bytes 6291456 | tf_op jit(solution)/shard_map/all_gather | solution.py:82
  7.3 231.9 %all-gather.10.cloned.1.call-start = ((), (), s32[]{:S(2)}) async-start(), calls=%async_computation.4 | async-start | bytes 8912896 | tf_op jit(solution)/shard_map/all_gather | solution.py:93
  8.0 502.1 %all-gather.6.cloned.1.call-start = ((), (), s32[]{:S(2)}) async-start(), calls=%async_computation.2 | async-start | bytes 71303168 | tf_op jit(solution)/shard_map/all_gather | solution.py:92
  8.7 633.1 %all-gather.14.cloned.1.call-start = ((), (), s32[]{:S(2)}) async-start(), calls=%async_computation.6 | async-start | bytes 4456448 | tf_op jit(solution)/shard_map/all_gather | solution.py:124
  8.8 8.8 collective-permute-start
  17.6 134.8 %copy-start.2 = (bf16[512,512]{1,0:T(8,128)(2,1)}, bf16[512,512]{1,0:T(8,128)(2,1)S(1)}, u32[]{:S(2)}) copy-start(bf16[512,512]{1,0:T(8,128)(2,1)S(1)} %collective-permute-done) | copy-start | bytes 1572868
  17.6 8.6 collective-permute-start.1
  26.2 126.2 %copy-start.6 = (bf16[512,512]{1,0:T(8,128)(2,1)}, bf16[512,512]{1,0:T(8,128)(2,1)S(1)}, u32[]{:S(2)}) copy-start(bf16[512,512]{1,0:T(8,128)(2,1)S(1)} %collective-permute-done.1) | copy-start | bytes 1572868
  26.2 8.6 collective-permute-start.2
  34.8 117.6 %copy-start.9 = (bf16[512,512]{1,0:T(8,128)(2,1)}, bf16[512,512]{1,0:T(8,128)(2,1)S(1)}, u32[]{:S(2)}) copy-start(bf16[512,512]{1,0:T(8,128)(2,1)S(1)} %collective-permute-done.2) | copy-start | bytes 1572868
  34.8 10.4 collective-permute-start.3
  45.2 54.4 %copy-start.12 = (bf16[512,512]{1,0:T(8,128)(2,1)}, bf16[512,512]{1,0:T(8,128)(2,1)S(1)}, u32[]{:S(2)}) copy-start(bf16[512,512]{1,0:T(8,128)(2,1)S(1)} %collective-permute-done.3) | copy-start | bytes 1572868
  45.2 11.3 collective-permute-start.4
  56.5 11.3 copy-start.13
  56.5 11.3 collective-permute-start.5
  67.8 11.3 collective-permute-start.6
  79.1 20.5 %collective-permute-start.7 = (bf16[512,512]{1,0:T(8,128)(2,1)S(1)}, bf16[512,512]{1,0:T(8,128)(2,1)S(1)}, u32[]{:S(2)}, u32[]{:S(2)}) collective-permute-start(bf16[512,512]{1,0:T(8,128)(2,1)S(1)} %collective-permute-done.6), channel_id=1, source_target_pairs={{0,2},{2,4},{4,6},{6,8},{8,10},{10,12},{12,14},{14,16},{16,18},{18... | collective-permute-start | bytes 1572872 | tf_op jit(solution)/shard_map/ppermute | solution.py:26
  99.6 13.4 %copy-start.4 = (bf16[512,512]{1,0:T(8,128)(2,1)}, bf16[512,512]{1,0:T(8,128)(2,1)S(1)}, u32[]{:S(2)}) copy-start(bf16[512,512]{1,0:T(8,128)(2,1)S(1)} %collective-permute-done.7) | copy-start | bytes 1572868
  99.6 13.4 %collective-permute-start.8 = (bf16[512,512]{1,0:T(8,128)(2,1)S(1)}, bf16[512,512]{1,0:T(8,128)(2,1)S(1)}, u32[]{:S(2)}, u32[]{:S(2)}) collective-permute-start(bf16[512,512]{1,0:T(8,128)(2,1)S(1)} %collective-permute-done.7), channel_id=1, source_target_pairs={{0,2},{2,4},{4,6},{6,8},{8,10},{10,12},{12,14},{14,16},{16,18},{18... | collective-permute-start | bytes 1572872 | tf_op jit(solution)/shard_map/ppermute | solution.py:26
  113.0 22.6 %copy-start.7 = (bf16[512,512]{1,0:T(8,128)(2,1)}, bf16[512,512]{1,0:T(8,128)(2,1)S(1)}, u32[]{:S(2)}) copy-start(bf16[512,512]{1,0:T(8,128)(2,1)S(1)} %collective-permute-done.8) | copy-start | bytes 1572868
  113.0 22.6 %collective-permute-start.9 = (bf16[512,512]{1,0:T(8,128)(2,1)S(1)}, bf16[512,512]{1,0:T(8,128)(2,1)S(1)}, u32[]{:S(2)}, u32[]{:S(2)}) collective-permute-start(bf16[512,512]{1,0:T(8,128)(2,1)S(1)} %collective-permute-done.8), channel_id=1, source_target_pairs={{0,2},{2,4},{4,6},{6,8},{8,10},{10,12},{12,14},{14,16},{16,18},{18... | collective-permute-start | bytes 1572872 | tf_op jit(solution)/shard_map/ppermute | solution.py:26
  135.6 16.9 %copy-start.10 = (bf16[512,512]{1,0:T(8,128)(2,1)}, bf16[512,512]{1,0:T(8,128)(2,1)S(1)}, u32[]{:S(2)}) copy-start(bf16[512,512]{1,0:T(8,128)(2,1)S(1)} %collective-permute-done.9) | copy-start | bytes 1572868
  135.6 16.8 %collective-permute-start.10 = (bf16[512,512]{1,0:T(8,128)(2,1)S(1)}, bf16[512,512]{1,0:T(8,128)(2,1)S(1)}, u32[]{:S(2)}, u32[]{:S(2)}) collective-permute-start(bf16[512,512]{1,0:T(8,128)(2,1)S(1)} %collective-permute-done.9), channel_id=1, source_target_pairs={{0,2},{2,4},{4,6},{6,8},{8,10},{10,12},{12,14},{14,16},{16,18},{18... | collective-permute-start | bytes 1572872 | tf_op jit(solution)/shard_map/ppermute | solution.py:26
  152.4 14.4 %collective-permute-start.11 = (bf16[512,512]{1,0:T(8,128)(2,1)S(1)}, bf16[512,512]{1,0:T(8,128)(2,1)S(1)}, u32[]{:S(2)}, u32[]{:S(2)}) collective-permute-start(bf16[512,512]{1,0:T(8,128)(2,1)S(1)} %collective-permute-done.10), channel_id=1, source_target_pairs={{0,2},{2,4},{4,6},{6,8},{8,10},{10,12},{12,14},{14,16},{16,18},{18... | collective-permute-start | bytes 1572872 | tf_op jit(solution)/shard_map/ppermute | solution.py:26
  152.7 21.3 %copy-start.3 = (bf16[512,512]{1,0:T(8,128)(2,1)S(1)}, bf16[512,512]{1,0:T(8,128)(2,1)}, u32[]{:S(2)}) copy-start(bf16[512,512]{1,0:T(8,128)(2,1)} %copy-done.2) | copy-start | bytes 1572868
  166.8 17.0 %collective-permute-start.12 = (bf16[512,512]{1,0:T(8,128)(2,1)S(1)}, bf16[512,512]{1,0:T(8,128)(2,1)}, u32[]{:S(2)}, u32[]{:S(2)}) collective-permute-start(bf16[512,512]{1,0:T(8,128)(2,1)S(1)} %collective-permute-done.11), channel_id=1, source_target_pairs={{0,2},{2,4},{4,6},{6,8},{8,10},{10,12},{12,14},{14,16},{16,18},{18... | collective-permute-start | bytes 1572872 | tf_op jit(solution)/shard_map/ppermute | solution.py:26
  179.4 8.0 copy-start.5
  183.8 22.8 %collective-permute-start.13 = (bf16[512,512]{1,0:T(8,128)(2,1)}, bf16[512,512]{1,0:T(8,128)(2,1)}, u32[]{:S(2)}, u32[]{:S(2)}) collective-permute-start(bf16[512,512]{1,0:T(8,128)(2,1)} %collective-permute-done.12), channel_id=1, source_target_pairs={{0,2},{2,4},{4,6},{6,8},{8,10},{10,12},{12,14},{14,16},{16,18},{18... | collective-permute-start | bytes 1572872 | tf_op jit(solution)/shard_map/ppermute | solution.py:26
  185.4 3.1 copy-start.8
  186.5 3.1 copy-start.11
  206.6 22.7 %collective-permute-start.14 = (bf16[512,512]{1,0:T(8,128)(2,1)}, bf16[512,512]{1,0:T(8,128)(2,1)S(1)}, u32[]{:S(2)}, u32[]{:S(2)}) collective-permute-start(bf16[512,512]{1,0:T(8,128)(2,1)} %collective-permute-done.13), channel_id=1, source_target_pairs={{0,2},{2,4},{4,6},{6,8},{8,10},{10,12},{12,14},{14,16},{16,18},{18... | collective-permute-start | bytes 1572872 | tf_op jit(solution)/shard_map/ppermute | solution.py:26
  238.5 409.6 %all-gather.12.cloned.1.call-start = ((), (), s32[]{:S(2)}) async-start(), calls=%async_computation.5 | async-start | bytes 4456448 | tf_op jit(solution)/shard_map/all_gather | solution.py:123
  631.2 43.4 %all-to-all-start = ((bf16[32,256,128]{1,2,0:T(8,128)(2,1)}), bf16[32,256,128]{1,2,0:T(8,128)(2,1)S(1)}, u32[]{:S(2)}, u32[]{:S(2)}) async-start(bf16[32,256,128]{1,2,0:T(8,128)(2,1)} %pad_maximum_fusion), calls=%async_computation | async-start | bytes 4194304 | tf_op jit(solution)/shard_map/all_to_all | solution.py:102
  933.1 1.7 copy-start
Sparse Core Ops, SparseCore 0:
  8.9 58.8 all-gather.7
  69.9 88.4 all-gather.9
  160.0 350.0 all-gather.5
  512.1 50.4 all-gather.13
  564.6 51.3 all-gather.11
